TPU v7x, 256 devices: a whole 4x4x8 slice. The times are simulated.
256 devices in a mesh: var: 8 (over y, core), tok: 32 (over x, z).
Axes of the slice: x: 4, y: 4, z: 8, core: 2. Of those that a mesh axis runs over, the one named last changes fastest.
Arguments:
- patches: bfloat16 [72, 4, 4096], P('var', None, 'tok'), may hold values from -6 to 6
- slot_var: int32 [72], replicated, may hold values from -1 to 47, as said below
- patch_weight: bfloat16 [48, 4, 1024], replicated, may hold values from -3 to 3
- var_embed: bfloat16 [48, 1024], replicated, may hold values from -6 to 6
- query: bfloat16 [1024], replicated, may hold values from -16 to 16
- key_weight: bfloat16 [1024, 1024], P('tok'), may hold values from -0.1875 to 0.1875
- value_weight: bfloat16 [1024, 1024], P('tok'), may hold values from -0.1875 to 0.1875
- out_weight: bfloat16 [1024, 1024], P('tok'), may hold values from -0.1875 to 0.1875
- cotangent: bfloat16 [4096, 1024], P(('tok', 'var')), may hold values from -6 to 6
Outputs:
- aggregated: bfloat16 [4096, 1024], P(('tok', 'var'))
- patch_grad: float32 [72, 4096], P('var', 'tok')
Inputs may be any that keep to these rules, and one draw needn't show every extreme that they name: `slot_var`: slot 9 * i + j belongs to index i of var. Every variable id stands in exactly one slot; empty slots hold -1. The live slots of an index come first and hold consecutive ids, rising from index to index. Every index holds at least one and at most 9 live slots, and some index holds exactly 9.
All inputs are finite; a program needn't handle non-finite values.
Results may differ from a plain program's by a relative error of at most 0.011.
Values may be sent and summed in bfloat16 or wider, within the bound.
No kernel may reach another device: no remote copies, remote signals or barrier semaphores. Data moves between devices by JAX's collectives and lax.ppermute only.
A program may use at most 128 MiB of HBM per device.

v0:
```python
import math
import jax
import jax.numpy as jnp
from jax import lax
from jax.sharding import PartitionSpec as P

H = 16
HD = 64
score_cap = 5.0
inv_sqrt_two = 1.0 / math.sqrt(2.0)
inv_sqrt_two_pi = 1.0 / math.sqrt(2.0 * math.pi)


def gelu_exact(inputs):
    return 0.5 * inputs * (1.0 + lax.erf(inputs * inv_sqrt_two))


def gelu_slope(inputs):
    return (
        0.5 * (1.0 + lax.erf(inputs * inv_sqrt_two))
        + inputs * jnp.exp(-0.5 * inputs * inputs) * inv_sqrt_two_pi
    )


def live_index(slot_var, var_total):
    ids = jnp.arange(var_total, dtype=jnp.int32)
    places = jnp.arange(slot_var.shape[0], dtype=jnp.int32)
    match = slot_var[None, :] == ids[:, None]
    return jnp.sum(jnp.where(match, places[None, :], 0), axis=1)


def attend(embedded, query, key_matrix, value_matrix, out_matrix, cot_rows):
    var_count, tok_count, width = embedded.shape
    flat_rows = embedded.reshape(var_count * tok_count, width)
    key_heads = (
        jnp.dot(flat_rows, key_matrix, preferred_element_type=jnp.float32)
        .astype(jnp.bfloat16)
        .reshape(var_count, tok_count, H, HD)
    )
    value_heads = (
        jnp.dot(flat_rows, value_matrix, preferred_element_type=jnp.float32)
        .astype(jnp.bfloat16)
        .reshape(var_count, tok_count, H, HD)
    )
    query_heads = query.reshape(H, HD)
    raw_scores = jnp.einsum(
        "vthj,hj->tvh", key_heads, query_heads, preferred_element_type=jnp.float32
    ) / math.sqrt(HD)
    squashed = jnp.tanh(raw_scores / score_cap)
    exp_scores = jnp.exp(score_cap * squashed)
    attn_f32 = exp_scores / jnp.sum(exp_scores, axis=1, keepdims=True)
    attn_bf = attn_f32.astype(jnp.bfloat16)
    pooled = (
        jnp.einsum("tvh,vthj->thj", attn_bf, value_heads, preferred_element_type=jnp.float32)
        .astype(jnp.bfloat16)
        .reshape(tok_count, width)
    )
    mixed_out = jnp.dot(pooled, out_matrix, preferred_element_type=jnp.float32).astype(jnp.bfloat16)
    contract = (((1,), (1,)), ((), ()))
    grad_pooled = (
        lax.dot_general(cot_rows, out_matrix, contract, preferred_element_type=jnp.float32)
        .astype(jnp.bfloat16)
        .reshape(tok_count, H, HD)
    )
    grad_attn = jnp.einsum(
        "thj,vthj->tvh", grad_pooled, value_heads, preferred_element_type=jnp.float32
    )
    attn_vth = jnp.transpose(attn_bf, (1, 0, 2)).astype(jnp.float32)
    grad_values = (attn_vth[:, :, :, None] * grad_pooled.astype(jnp.float32)[None]).astype(
        jnp.bfloat16
    )
    grad_scores = attn_f32 * (grad_attn - jnp.sum(attn_f32 * grad_attn, axis=1, keepdims=True))
    grad_raw = grad_scores * (1.0 - squashed * squashed) / math.sqrt(HD)
    query_f32 = query_heads.astype(jnp.float32)
    grad_keys = (jnp.transpose(grad_raw, (1, 0, 2))[:, :, :, None] * query_f32[None, None]).astype(
        jnp.bfloat16
    )
    grad_embed = lax.dot_general(
        grad_keys.reshape(var_count * tok_count, width),
        key_matrix,
        contract,
        preferred_element_type=jnp.float32,
    )
    grad_embed = grad_embed + lax.dot_general(
        grad_values.reshape(var_count * tok_count, width),
        value_matrix,
        contract,
        preferred_element_type=jnp.float32,
    )
    return (mixed_out, grad_embed.astype(jnp.bfloat16).reshape(var_count, tok_count, width))


def body(
    patches,
    slot_var,
    patch_weight,
    var_embed,
    query,
    key_weight,
    value_weight,
    out_weight,
    cotangent,
):
    var_total, _, width = patch_weight.shape
    local_slots = patches.shape[0]
    live_slot = live_index(slot_var, var_total)
    key_matrix, value_matrix = (
        lax.all_gather(key_weight, "tok", axis=0, tiled=True),
        lax.all_gather(value_weight, "tok", axis=0, tiled=True),
    )
    out_matrix = lax.all_gather(out_weight, "tok", axis=0, tiled=True)
    first_slot = lax.axis_index("var") * local_slots
    own_vars = lax.dynamic_slice_in_dim(slot_var, first_slot, local_slots)
    picker = (own_vars[:, None] == jnp.arange(var_total, dtype=jnp.int32)[None, :]).astype(
        jnp.bfloat16
    )
    slot_table = (
        jnp.dot(
            picker, patch_weight.reshape(var_total, 4 * width), preferred_element_type=jnp.float32
        )
        .astype(jnp.bfloat16)
        .reshape(local_slots, 4, width)
    )
    slot_shift = jnp.dot(picker, var_embed, preferred_element_type=jnp.float32)
    pre_act = (
        jnp.einsum("spt,spd->std", patches, slot_table, preferred_element_type=jnp.float32)
        + slot_shift[:, None, :]
    )
    embedded = gelu_exact(pre_act).astype(jnp.bfloat16)
    spread = lax.all_to_all(embedded, "var", split_axis=1, concat_axis=0, tiled=True)
    live_rows = jnp.take(spread, live_slot, axis=0)
    mixed_out, grad_embed = attend(
        live_rows, query, key_matrix, value_matrix, out_matrix, cotangent
    )
    grad_slots = jnp.zeros(spread.shape, jnp.bfloat16).at[live_slot].set(grad_embed)
    returned = lax.all_to_all(grad_slots, "var", split_axis=0, concat_axis=1, tiled=True)
    grad_pre = returned.astype(jnp.float32) * gelu_slope(pre_act)
    slot_grad = jnp.einsum(
        "spt,std->spd", patches.astype(jnp.float32), grad_pre, precision=lax.Precision.HIGHEST
    ).reshape(local_slots, 4 * width)
    grad_out = lax.psum_scatter(slot_grad, "tok", scatter_dimension=1, tiled=True)
    return (mixed_out, grad_out)


def solution(mesh):
    return jax.shard_map(
        body,
        mesh=mesh,
        in_specs=(
            P("var", None, "tok"),
            P(),
            P(),
            P(),
            P(),
            P("tok", None),
            P("tok", None),
            P("tok", None),
            P(("tok", "var"), None),
        ),
        out_specs=(P(("tok", "var"), None), P("var", "tok")),
        check_vma=False,
    )
```

profile of v0, /device:TPU:8, one launch (start us, length us, event | category | flops | bytes accessed | tf_op | source)
XLA Modules:
  0.0 545.3 jit_solution(2519850298434397522)
XLA Ops:
  7.2 0.7 all-gather.8.cloned.1.call-update
  8.0 0.7 all-gather.6.cloned.1.call-update
  8.7 0.7 all-gather.4.cloned.1.call-update
  9.4 1.1 copy.47
  10.5 0.7 dynamic_slice.3
  11.3 0.2 convolution_convert_fusion
  11.6 0.2 fusion.30
  11.8 4.6 fusion.6
  16.3 6.6 %copy.29 = bf16[9,128,1024]{2,0,1:T(8,128)(2,1)} copy(bf16[9,128,1024]{1,2,0:T(8,128)(2,1)S(1)} %get-tuple-element.6) | data formatting | bytes 4718592 | tf_op jit(solution)/shard_map/convert_element_type | solution.py:129
  22.9 6.7 %all-to-all-start = ((bf16[9,128,1024]{2,0,1:T(8,128)(2,1)}), bf16[9,128,1024]{2,0,1:T(8,128)(2,1)}, u32[]{:S(2)}, u32[]{:S(2)}) async-start(bf16[9,128,1024]{2,0,1:T(8,128)(2,1)} %copy.29), calls=%async_computation | async-start | bytes 8388608 | tf_op jit(solution)/shard_map/all_to_all | solution.py:130
  30.1 47.9 %all-to-all-done = bf16[9,128,1024]{2,0,1:T(8,128)(2,1)} async-done(((bf16[9,128,1024]{2,0,1:T(8,128)(2,1)}), bf16[9,128,1024]{2,0,1:T(8,128)(2,1)}, u32[]{:S(2)}, u32[]{:S(2)}) %all-to-all-start) | async-done | bytes 2359328 | tf_op jit(solution)/shard_map/all_to_all | solution.py:130
  78.0 3.7 copy.31
  81.7 1.9 gather_fusion
  83.6 1.6 bitcast_select_fusion
  85.3 6.1 %all-gather.8.cloned.1.call-done = bf16[1024,1024]{1,0:T(8,128)(2,1)} async-done(((bf16[32,1024]{1,0:T(8,128)(2,1)}), bf16[1024,1024]{1,0:T(8,128)(2,1)}) %all-gather.8.cloned.1.call-update) | async-done | bytes 2097168 | tf_op jit(solution)/shard_map/all_gather | solution.py:111
  91.4 2.2 convolution_convert_fusion.3
  93.6 0.1 reshape.117
  93.9 75.1 %all-gather.6.cloned.1.call-done = bf16[1024,1024]{1,0:T(8,128)(2,1)} async-done(((bf16[32,1024]{1,0:T(8,128)(2,1)}), bf16[1024,1024]{1,0:T(8,128)(2,1)}) %all-gather.6.cloned.1.call-update) | async-done | bytes 2097168 | tf_op jit(solution)/shard_map/all_gather | solution.py:109
  168.9 4.6 convolution_convert_fusion.1
  173.5 4.1 reshape.85
  177.6 69.0 %all-gather.4.cloned.1.call-done = bf16[1024,1024]{1,0:T(8,128)(2,1)} async-done(((bf16[32,1024]{1,0:T(8,128)(2,1)}), bf16[1024,1024]{1,0:T(8,128)(2,1)}) %all-gather.4.cloned.1.call-update) | async-done | bytes 2097168 | tf_op jit(solution)/shard_map/all_gather | solution.py:108
  246.7 5.0 convolution_convert_fusion.2
  251.7 5.2 reshape.83
  256.9 5.3 fusion.12
  262.2 0.2 bitcast_reduce_fusion
  262.4 1.9 fusion.14
  264.4 0.2 multiply_reduce_fusion
  264.6 0.1 convert_convert_fusion
  264.7 0.2 copy.32
  264.9 3.8 mul.100
  268.8 6.3 %mul.101 = f32[768,1024]{1,0:T(8,128)} reshape(f32[48,16,16,64]{3,2,1,0:T(8,128)} %mul.100) | data formatting | bytes 6291456 | tf_op jit(solution)/shard_map/mul | solution.py:75
  275.1 1.0 copy.33
  276.1 3.3 multiply_convert_fusion
  279.4 3.2 convert_element_type.86
  282.6 4.5 fusion.22
  287.1 3.0 add_convert_fusion
  290.1 0.3 broadcast_in_dim.48
  290.4 5.1 scatter_fusion
  295.5 33.5 %all_to_all.27 = bf16[72,16,1024]{2,1,0:T(8,128)(2,1)S(1)} all-to-all(bf16[72,16,1024]{2,1,0:T(8,128)(2,1)S(1)} %scatter_fusion), channel_id=1, replica_groups=mesh['var'=8,'tok'=32] {'var'}, dimensions={0} | all-to-all | bytes 4718592 | tf_op jit(solution)/shard_map/all_to_all | solution.py:136
  329.0 0.6 convert_bitcast_fusion
  329.6 2.8 copy.34
  332.4 6.0 %copy.35 = f32[9,128,1024]{1,2,0:T(8,128)} copy(f32[9,128,1024]{2,1,0:T(8,128)} %bitcast.116) | data formatting | bytes 9437184 | tf_op jit(solution)/shard_map/convert_element_type | solution.py:137
  338.5 6.8 %fusion.24 = f32[9,4,1024]{2,1,0:T(4,128)S(1)} fusion(bf16[9,4,128]{2,1,0:T(4,128)(2,1)S(1)} %copy-done.7, f32[9,128,1024]{1,2,0:T(8,128)} %copy.35, f32[9,1024,128]{2,1,0:T(8,128)} %get-tuple-element.7, f32[9,1024]{1,0:T(8,128)S(1)} %fusion.30), kind=kOutput, calls=%fused_computation.36 | convolution fusion | flops 68419584 | bytes 9630720 | tf_op jit(solution)/shard_map/spt,std->spd/dot_general | solution.py:138
  345.4 0.9 copy.48
  346.3 3.8 fusion.16
  350.1 0.1 reshape.86
  350.2 1.0 convolution_convert_fusion.4
  351.2 187.6 %reduce-scatter.2.cloned.1.call-done = f32[9,128]{1,0:T(8,128)} async-done(((f32[9,4096]{1,0:T(8,128)}), f32[9,128]{1,0:T(8,128)}) %reduce-scatter.2.cloned.1.call-update) | async-done | bytes 4624 | tf_op jit(solution)/shard_map/reduce_scatter | solution.py:141
  (40 shorter events, 0.8 us)
Async XLA Ops:
  7.2 4.4 copy-start
  7.2 84.2 %all-gather.8.cloned.1.call-start = ((), (), s32[]{:S(2)}) async-start(), calls=%async_computation.5 | async-start | bytes 2162688 | tf_op jit(solution)/shard_map/all_gather | solution.py:111
  7.9 161.0 %all-gather.6.cloned.1.call-start = ((), (), s32[]{:S(2)}) async-start(), calls=%async_computation.4 | async-start | bytes 2162688 | tf_op jit(solution)/shard_map/all_gather | solution.py:109
  8.7 238.0 %all-gather.4.cloned.1.call-start = ((), (), s32[]{:S(2)}) async-start(), calls=%async_computation.3 | async-start | bytes 2162688 | tf_op jit(solution)/shard_map/all_gather | solution.py:108
  22.9 6.7 %copy-start.8 = (bf16[1024]{0:T(1024)(128)(2,1)S(1)}, bf16[1024]{0:T(1024)(128)(2,1)}, u32[]{:S(2)}) copy-start(bf16[1024]{0:T(1024)(128)(2,1)} %param.13) | copy-start | bytes 6148
  22.9 6.8 %copy-start.10 = (s32[72]{0:T(128)S(1)}, s32[72]{0:T(128)}, u32[]{:S(2)}) copy-start(s32[72]{0:T(128)} %param.10) | copy-start | bytes 868
  22.9 55.1 %all-to-all-start = ((bf16[9,128,1024]{2,0,1:T(8,128)(2,1)}), bf16[9,128,1024]{2,0,1:T(8,128)(2,1)}, u32[]{:S(2)}, u32[]{:S(2)}) async-start(bf16[9,128,1024]{2,0,1:T(8,128)(2,1)} %copy.29), calls=%async_computation | async-start | bytes 8388608 | tf_op jit(solution)/shard_map/all_to_all | solution.py:130
  29.6 509.1 %reduce-scatter.2.cloned.1.call-start = ((), (), s32[]{:S(2)}) async-start(), calls=%async_computation.6 | async-start | bytes 270336 | tf_op jit(solution)/shard_map/reduce_scatter | solution.py:141
  81.7 9.7 %copy-start.6 = (bf16[16,1024]{1,0:T(8,128)(2,1)S(1)}, bf16[16,1024]{1,0:T(8,128)(2,1)}, u32[]{:S(2)}) copy-start(bf16[16,1024]{1,0:T(8,128)(2,1)} %param.17) | copy-start | bytes 98308
  85.2 83.7 %copy-start.4 = (bf16[768,1024]{1,0:T(8,128)(2,1)}, bf16[768,1024]{1,0:T(8,128)(2,1)S(1)}, u32[]{:S(2)}) copy-start(bf16[768,1024]{1,0:T(8,128)(2,1)S(1)} %bitcast_select_fusion) | copy-start | bytes 4718596
  177.6 84.8 %copy-start.3 = (bf16[48,16,16,64]{3,2,1,0:T(8,128)(2,1)}, bf16[48,16,16,64]{3,2,1,0:T(8,128)(2,1)S(1)}, u32[]{:S(2)}) copy-start(bf16[48,16,16,64]{3,2,1,0:T(8,128)(2,1)S(1)} %reshape.85) | copy-start | bytes 4718596
  282.6 4.5 copy-start.5
  282.6 4.5 copy-start.9
  332.4 6.1 %copy-start.7 = (bf16[9,4,128]{2,1,0:T(4,128)(2,1)S(1)}, bf16[9,4,128]{2,1,0:T(4,128)(2,1)}, u32[]{:S(2)}) copy-start(bf16[9,4,128]{2,1,0:T(4,128)(2,1)} %param.9) | copy-start | bytes 27652
  345.3 4.9 copy-start.2
  346.3 192.5 %copy-start.1 = (bf16[48,1024]{1,0:T(8,128)(2,1)S(1)}, bf16[48,1024]{1,0:T(8,128)(2,1)}, u32[]{:S(2)}) copy-start(bf16[48,1024]{1,0:T(8,128)(2,1)} %param.12) | copy-start | bytes 294916
Sparse Core Ops, SparseCore 0:
  10.6 80.7 all-gather.7
  94.0 74.9 all-gather.5
  171.5 75.0 all-gather.3
  346.4 192.3 reduce-scatter.1
where the time goes:
time: 546 us; the launch traced here: 545 us
  waiting for transfers between devices  388 us (71%)
  local copies, waits for them, and re-layouts  53.8 us (10%)
  matrix products  43.2 us (8%)
  blocking collectives  33.5 us (6%)
  between operations  14 us (3%)
  starting transfers between devices  6.85 us (1%)
  other arithmetic  6.17 us (1%)
    reduce_scatter x1, waiting for transfers between devices, body(): lax.psum_scatter(slot_grad, 'tok', scatter_dimension=1, tiled=True)  188 us
    all_gather x1, waiting for transfers between devices, body(): lax.all_gather(value_weight, 'tok', axis=0, tiled=True)  75.1 us
    all_gather x1, waiting for transfers between devices, body(): lax.all_gather(key_weight, 'tok', axis=0, tiled=True)  69 us
    all_to_all x1, waiting for transfers between devices, body(): lax.all_to_all(embedded, 'var', split_axis=1, concat_axis=0, tiled=True)  47.9 us
    all_to_all x1, blocking collectives, body(): lax.all_to_all(grad_slots, 'var', split_axis=0, concat_axis=1, tiled=True)  33.5 us
  transfers between devices with their start and end apart: 5, of which 5 were waited for; matrix products, arithmetic and copies ran while one was open for 7% of the time, Pallas kernels for 0%

commit v1 on v0

--- a/solution.py
+++ b/solution.py
@@ -106,7 +106,9 @@
     live_slot = live_index(slot_var, var_total)
     key_matrix, value_matrix = (
         lax.all_gather(key_weight, "tok", axis=0, tiled=True),
-        lax.all_gather(value_weight, "tok", axis=0, tiled=True),
+        jnp.concatenate(
+            lax.all_to_all(jnp.stack([value_weight] * lax.axis_size("tok")), "tok", 0, 0), axis=0
+        ),
     )
     out_matrix = lax.all_gather(out_weight, "tok", axis=0, tiled=True)
     first_slot = lax.axis_index("var") * local_slots

time: 546 us -> 475 us (0.87)
  waiting for transfers between devices: 388 us -> 252 us
  blocking collectives: 33.5 us -> 89 us
    all_gather x1 -> x0, waiting for transfers between devices: 75.1 us -> none  [body(): lax.all_gather(value_weight, 'tok', axis=0, tiled=True)]
    all_to_all x0 -> x1, blocking collectives: none -> 55.5 us  [body(): lax.all_to_all(embedded, 'var', split_axis=1, concat_axis=0, tiled=True)]
    all_gather x1, waiting for transfers between devices: 69 us -> 23.7 us  [body(): lax.all_gather(key_weight, 'tok', axis=0, tiled=True)]
    all_to_all x1, waiting for transfers between devices: 47.9 us -> 39.6 us  [body(): lax.all_to_all(jnp.stack([value_weight] * lax.axis_size('tok')), 'tok', 0...]
    all_gather x1, waiting for transfers between devices: 6.11 us -> 0.01 us  [body(): out_matrix = lax.all_gather(out_weight, 'tok', axis=0, tiled=True)]
  transfers between devices with their start and end apart: 5 -> 4, of which waited for: 5 -> 3; matrix products, arithmetic and copies ran while one was open for 7% -> 9% of each run, Pallas kernels for 0% -> 0%
where the time goes in v1:
time: 475 us; the launch traced here: 474 us
  waiting for transfers between devices  252 us (53%)
  blocking collectives  89 us (19%)
  local copies, waits for them, and re-layouts  57.3 us (12%)
  matrix products  44.8 us (9%)
  between operations  14 us (3%)
  starting transfers between devices  9.94 us (2%)
  other arithmetic  6.19 us (1%)
    reduce_scatter x1, waiting for transfers between devices, body(): lax.psum_scatter(slot_grad, 'tok', scatter_dimension=1, tiled=True)  188 us
    all_to_all x1, blocking collectives, body(): lax.all_to_all(embedded, 'var', split_axis=1, concat_axis=0, tiled=True)  55.5 us
    all_to_all x1, waiting for transfers between devices, body(): lax.all_to_all(jnp.stack([value_weight] * lax.axis_size('tok')), 'tok', 0...  39.6 us
    all_to_all x1, blocking collectives, body(): lax.all_to_all(grad_slots, 'var', split_axis=0, concat_axis=1, tiled=True)  33.5 us
    all_gather x1, waiting for transfers between devices, body(): lax.all_gather(key_weight, 'tok', axis=0, tiled=True)  23.7 us
    mul x2, local copies, waits for them, and re-layouts, attend(): jnp.transpose(grad_raw, (1, 0, 2))[:, :, :, None] * query_f32[None, None]  10.1 us
    all_to_all x1, starting transfers between devices, body(): lax.all_to_all(jnp.stack([value_weight] * lax.axis_size('tok')), 'tok', 0...  9.83 us
  transfers between devices with their start and end apart: 4, of which 3 were waited for; matrix products, arithmetic and copies ran while one was open for 9% of the time, Pallas kernels for 0%

profile of v1, /device:TPU:8, one launch (start us, length us, event | category | flops | bytes accessed | tf_op | source)
XLA Modules:
  0.0 473.5 jit_solution(12397407487997968455)
XLA Ops:
  7.2 0.7 all-gather.5.cloned.1.call-update
  7.9 1.1 copy.47
  9.0 0.7 dynamic_slice.3
  9.8 0.2 convolution_convert_fusion
  10.1 0.2 fusion.30
  10.3 4.5 fusion.6
  14.8 6.6 %copy.29 = bf16[9,128,1024]{2,0,1:T(8,128)(2,1)} copy(bf16[9,128,1024]{1,2,0:T(8,128)(2,1)S(1)} %get-tuple-element.6) | data formatting | bytes 4718592 | tf_op jit(solution)/shard_map/convert_element_type | solution.py:131
  21.4 55.5 %all_to_all.32 = bf16[9,128,1024]{2,0,1:T(8,128)(2,1)} all-to-all(bf16[9,128,1024]{2,0,1:T(8,128)(2,1)} %copy.29), channel_id=1, replica_groups=mesh['var'=8,'tok'=32] {'var'}, dimensions={1} | all-to-all | bytes 4718592 | tf_op jit(solution)/shard_map/all_to_all | solution.py:132
  76.9 1.6 stack.2
  78.6 9.8 %all-to-all-start.1 = ((bf16[32,32,1024]{2,1,0:T(8,128)(2,1)}), bf16[32,32,1024]{2,1,0:T(8,128)(2,1)}, u32[]{:S(2)}, u32[]{:S(2)}) async-start(bf16[32,32,1024]{2,1,0:T(8,128)(2,1)} %stack.2), calls=%async_computation.1 | async-start | bytes 4194304 | tf_op jit(solution)/shard_map/all_to_all | solution.py:110
  88.4 0.7 all-gather.3.cloned.1.call-update
  89.6 5.1 %copy.31 = bf16[8,9,16,1024]{3,2,1,0:T(8,128)(2,1)} copy(bf16[8,9,16,1024]{3,1,2,0:T(8,128)(2,1)} %bitcast.119) | data formatting | bytes 4718592 | tf_op jit(solution)/shard_map/all_to_all | solution.py:132
  94.7 2.3 gather_fusion
  97.1 0.2 broadcast_select_fusion
  97.3 1.4 bitcast_select_fusion
  98.7 2.2 convolution_convert_fusion.3
  101.0 0.1 reshape.161
  101.2 39.6 %all-to-all-done.1 = bf16[32,32,1024]{2,1,0:T(8,128)(2,1)} async-done(((bf16[32,32,1024]{2,1,0:T(8,128)(2,1)}), bf16[32,32,1024]{2,1,0:T(8,128)(2,1)}, u32[]{:S(2)}, u32[]{:S(2)}) %all-to-all-start.1) | async-done | bytes 2097184 | tf_op jit(solution)/shard_map/all_to_all | solution.py:110
  140.8 4.5 convolution_convert_fusion.1
  145.3 4.1 reshape.129
  149.5 23.7 %all-gather.3.cloned.1.call-done = bf16[1024,1024]{1,0:T(8,128)(2,1)} async-done(((bf16[32,1024]{1,0:T(8,128)(2,1)}), bf16[1024,1024]{1,0:T(8,128)(2,1)}) %all-gather.3.cloned.1.call-update) | async-done | bytes 2097168 | tf_op jit(solution)/shard_map/all_gather | solution.py:108
  173.1 5.0 %convolution_convert_fusion.2 = bf16[768,1024]{1,0:T(8,128)(2,1)} fusion(bf16[768,1024]{1,0:T(8,128)(2,1)} %bitcast_select_fusion, bf16[1024,1024]{1,0:T(8,128)(2,1)} %all-gather.3.cloned.1.call-done), kind=kOutput, calls=%fused_computation.32 | convolution fusion | flops 1611399168 | bytes 5242880 | tf_op jit(solution)/shard_map/dot_general | solution.py:36
  178.1 5.2 %reshape.126 = bf16[48,16,16,64]{3,2,1,0:T(8,128)(2,1)} reshape(bf16[768,1024]{1,0:T(8,128)(2,1)} %convolution_convert_fusion.2) | data formatting | bytes 3145728 | tf_op jit(solution)/shard_map/reshape | solution.py:38
  183.4 5.3 %fusion.12 = f32[16,1,48,16]{2,1,3,0:T(1,128)S(1)} fusion(bf16[16,64,1,1]{1,2,3,0:T(2,128)(2,1)S(1)} %reshape.159, bf16[48,16,16,64]{3,2,1,0:T(8,128)(2,1)} %reshape.126), kind=kOutput, calls=%fused_computation.19 | convolution fusion | flops 1572864 | bytes 1624064 | tf_op jit(solution)/shard_map/vthj,hj->tvh/dot_general | solution.py:46
  188.7 0.2 bitcast_reduce_fusion
  188.9 1.9 fusion.14
  190.8 0.2 multiply_reduce_fusion
  191.1 0.1 convert_convert_fusion
  191.2 0.2 copy.32
  191.4 3.8 mul.106
  195.3 6.3 %mul.107 = f32[768,1024]{1,0:T(8,128)} reshape(f32[48,16,16,64]{3,2,1,0:T(8,128)} %mul.106) | data formatting | bytes 6291456 | tf_op jit(solution)/shard_map/mul | solution.py:75
  201.6 1.0 copy.33
  202.5 3.3 multiply_convert_fusion
  205.9 3.2 convert_element_type.92
  209.0 4.5 fusion.22
  213.5 4.7 add_convert_fusion
  218.2 0.3 broadcast_in_dim.54
  218.5 5.1 %scatter_fusion = bf16[72,16,1024]{2,1,0:T(8,128)(2,1)S(1)} fusion(bf16[72,16,1024]{2,1,0:T(8,128)(2,1)S(1)} %broadcast_in_dim.54, s32[48]{0:T(128)S(1)} %fusion.33, bf16[48,16,1024]{2,1,0:T(8,128)(2,1)} %bitcast.122), kind=kCustom, calls=%fused_computation.1 | custom fusion | bytes 4718784 | tf_op jit(solution)/shard_map/scatter | solution.py:137
  223.6 33.5 %all_to_all.33 = bf16[72,16,1024]{2,1,0:T(8,128)(2,1)S(1)} all-to-all(bf16[72,16,1024]{2,1,0:T(8,128)(2,1)S(1)} %scatter_fusion), channel_id=1, replica_groups=mesh['var'=8,'tok'=32] {'var'}, dimensions={0} | all-to-all | bytes 4718592 | tf_op jit(solution)/shard_map/all_to_all | solution.py:138
  257.0 0.6 convert_bitcast_fusion
  257.6 2.9 copy.34
  260.5 6.1 %copy.35 = f32[9,128,1024]{1,2,0:T(8,128)} copy(f32[9,128,1024]{2,1,0:T(8,128)} %bitcast.118) | data formatting | bytes 9437184 | tf_op jit(solution)/shard_map/convert_element_type | solution.py:139
  266.5 6.8 %fusion.24 = f32[9,4,1024]{2,1,0:T(4,128)S(1)} fusion(bf16[9,4,128]{2,1,0:T(4,128)(2,1)S(1)} %copy-done.7, f32[9,128,1024]{1,2,0:T(8,128)} %copy.35, f32[9,1024,128]{2,1,0:T(8,128)} %get-tuple-element.7, f32[9,1024]{1,0:T(8,128)S(1)} %fusion.30), kind=kOutput, calls=%fused_computation.37 | convolution fusion | flops 68419584 | bytes 9630720 | tf_op jit(solution)/shard_map/spt,std->spd/dot_general | solution.py:140
  273.4 0.9 copy.48
  274.3 3.8 fusion.16
  278.1 0.1 reshape.130
  278.3 1.0 convolution_convert_fusion.4
  279.3 187.7 %reduce-scatter.2.cloned.1.call-done = f32[9,128]{1,0:T(8,128)} async-done(((f32[9,4096]{1,0:T(8,128)}), f32[9,128]{1,0:T(8,128)}) %reduce-scatter.2.cloned.1.call-update) | async-done | bytes 4624 | tf_op jit(solution)/shard_map/reduce_scatter | solution.py:143
  (38 shorter events, 0.8 us)
Async XLA Ops:
  7.2 2.9 copy-start
  7.2 91.6 %all-gather.5.cloned.1.call-start = ((), (), s32[]{:S(2)}) async-start(), calls=%async_computation.5 | async-start | bytes 2162688 | tf_op jit(solution)/shard_map/all_gather | solution.py:113
  21.4 55.5 %copy-start.5 = (bf16[32,1024]{1,0:T(8,128)(2,1)S(1)}, bf16[32,1024]{1,0:T(8,128)(2,1)}, u32[]{:S(2)}) copy-start(bf16[32,1024]{1,0:T(8,128)(2,1)} %param.15) | copy-start | bytes 196612
  76.9 12.3 %copy-start.8 = (bf16[1024]{0:T(1024)(128)(2,1)S(1)}, bf16[1024]{0:T(1024)(128)(2,1)}, u32[]{:S(2)}) copy-start(bf16[1024]{0:T(1024)(128)(2,1)} %param.13) | copy-start | bytes 6148
  76.9 12.3 %copy-start.9 = (s32[72]{0:T(128)S(1)}, s32[72]{0:T(128)}, u32[]{:S(2)}) copy-start(s32[72]{0:T(128)} %param.10) | copy-start | bytes 868
  78.6 62.2 %all-to-all-start.1 = ((bf16[32,32,1024]{2,1,0:T(8,128)(2,1)}), bf16[32,32,1024]{2,1,0:T(8,128)(2,1)}, u32[]{:S(2)}, u32[]{:S(2)}) async-start(bf16[32,32,1024]{2,1,0:T(8,128)(2,1)} %stack.2), calls=%async_computation.1 | async-start | bytes 4194304 | tf_op jit(solution)/shard_map/all_to_all | solution.py:110
  88.4 84.7 %all-gather.3.cloned.1.call-start = ((), (), s32[]{:S(2)}) async-start(), calls=%async_computation.4 | async-start | bytes 2162688 | tf_op jit(solution)/shard_map/all_gather | solution.py:108
  89.2 377.9 %reduce-scatter.2.cloned.1.call-start = ((), (), s32[]{:S(2)}) async-start(), calls=%async_computation.6 | async-start | bytes 270336 | tf_op jit(solution)/shard_map/reduce_scatter | solution.py:143
  97.1 1.7 copy-start.6
  149.5 39.4 %copy-start.3 = (bf16[48,16,16,64]{3,2,1,0:T(8,128)(2,1)}, bf16[48,16,16,64]{3,2,1,0:T(8,128)(2,1)S(1)}, u32[]{:S(2)}) copy-start(bf16[48,16,16,64]{3,2,1,0:T(8,128)(2,1)S(1)} %reshape.129) | copy-start | bytes 4718596
  209.0 4.5 copy-start.4
  260.5 6.1 %copy-start.7 = (bf16[9,4,128]{2,1,0:T(4,128)(2,1)S(1)}, bf16[9,4,128]{2,1,0:T(4,128)(2,1)}, u32[]{:S(2)}) copy-start(bf16[9,4,128]{2,1,0:T(4,128)(2,1)} %param.9) | copy-start | bytes 27652
  273.4 4.9 %copy-start.2 = (bf16[1024,1024]{1,0:T(8,128)(2,1)S(1)}, bf16[1024,1024]{1,0:T(8,128)(2,1)}, u32[]{:S(2)}) copy-start(bf16[1024,1024]{1,0:T(8,128)(2,1)} %all-gather.5.cloned.1.call-done) | copy-start | bytes 6291460
  274.3 192.7 %copy-start.1 = (bf16[48,1024]{1,0:T(8,128)(2,1)S(1)}, bf16[48,1024]{1,0:T(8,128)(2,1)}, u32[]{:S(2)}) copy-start(bf16[48,1024]{1,0:T(8,128)(2,1)} %param.12) | copy-start | bytes 294916
Sparse Core Ops, SparseCore 0:
  10.6 80.9 all-gather.4
  94.1 78.9 all-gather.2
  274.4 192.5 reduce-scatter.1
